TPU v7x, 32 devices: a whole 2x2x4 slice. The times are simulated.
32 devices in a mesh: img: 8 (over z, core), slab: 4 (over y, x).
Axes of the slice: x: 2, y: 2, z: 4, core: 2. Of those that a mesh axis runs over, the one named last changes fastest.
Arguments:
- image_masses: float32 [8, 3072, 3072], P('img', 'slab'), may hold values from 0.1 to 10
- dual_multipliers: float32 [8, 3072, 3072], P('img', 'slab'), may hold values from 0.1 to 10
- fraction_tops: int32 [8], P('img'), may hold values from 1 to 8
- banded_submatrices: bfloat16 [24, 3, 128, 128], replicated, as said below
- band_starts: int32 [24, 3], replicated, may hold values from -2 to 2, as said below
Outputs:
- barycenter: float32 [3072, 3072], P('slab')
- new_scalings: float32 [8, 3072, 3072], P('img', 'slab')
Inputs may be any that keep to these rules, and one draw needn't show every extreme that they name: `band_starts`: each row of offsets holds three consecutive numbers in increasing order; the first row is 0, 1, 2 and the last row is -2, -1, 0. `banded_submatrices`: all entries are positive.
All inputs are finite; a program needn't handle non-finite values.
Results may differ from a plain program's by a relative error of at most 0.0032.
Values may be sent and summed in bfloat16 or wider, within the bound.
No kernel may reach another device: no remote copies, remote signals or barrier semaphores. Data moves between devices by JAX's collectives and lax.ppermute only.
A program may use at most 192 MiB of HBM per device.

v0:
```python
import jax
import jax.numpy as jnp
from jax import lax
from jax.sharding import PartitionSpec as P

ITERS = 2


def offset_terms(banded_submatrices, band_starts):
    offsets = jnp.arange(-2, 3, dtype=jnp.int32)
    matches = band_starts[:, None, :] == offsets[None, :, None]
    picked = jnp.where(
        matches[:, :, :, None, None], banded_submatrices[:, None], jnp.zeros((), jnp.bfloat16)
    )
    return jnp.sum(picked, axis=2)


def column_sweep(field, terms):
    block_stack = terms.shape[0]
    width = terms.shape[2]
    count = field.shape[0]
    height = field.shape[1]
    leading = field.reshape((count * height, block_stack, width)).transpose(1, 0, 2)
    padded = jnp.pad(leading, ((2, 2), (0, 0), (0, 0)))
    total = jnp.zeros((block_stack, count * height, width), jnp.float32)
    for offset in range(5):
        total = total + lax.dot_general(
            padded[offset : offset + block_stack],
            terms[:, offset],
            (((2,), (2,)), ((0,), (0,))),
            preferred_element_type=jnp.float32,
        )
    return total.transpose(1, 0, 2).reshape((count, height, block_stack * width))


def rows_pass(padded, terms):
    block_stack = terms.shape[0]
    width = terms.shape[2]
    columns = padded.shape[2]
    split = padded[0].reshape((block_stack + 4, width, columns))
    total = jnp.zeros((block_stack, width, columns), jnp.float32)
    for offset in range(5):
        total = total + lax.dot_general(
            terms[:, offset],
            split[offset : offset + block_stack],
            (((2,), (1,)), ((0,), (0,))),
            preferred_element_type=jnp.float32,
        )
    outputs = [total.reshape((block_stack * width, columns))]
    return jnp.stack(outputs, axis=0)


def per_device(image_masses, dual_multipliers, fraction_tops, banded_submatrices, band_starts):
    width = banded_submatrices.shape[2]
    terms = offset_terms(banded_submatrices, band_starts)
    total_weight = lax.psum(jnp.sum(fraction_tops).astype(jnp.float32), "img")
    weights = fraction_tops.astype(jnp.float32)

    def apply_kernel(field):
        inner = column_sweep(field, terms).astype(jnp.bfloat16)
        columns = lax.all_to_all(inner, "slab", split_axis=2, concat_axis=1, tiled=True)
        padded = jnp.pad(columns, ((0, 0), (2 * width, 2 * width), (0, 0)))
        result = rows_pass(padded, terms).astype(jnp.bfloat16)
        return lax.all_to_all(result, "slab", split_axis=1, concat_axis=2, tiled=True)

    latest_multiplier = dual_multipliers
    barycenter = jnp.zeros(image_masses.shape[1:], jnp.float32)
    for iteration in range(ITERS):
        kernel_v = apply_kernel(latest_multiplier.astype(jnp.bfloat16))
        scaled_u = (image_masses / kernel_v.astype(jnp.float32)).astype(jnp.bfloat16)
        kernel_u = apply_kernel(scaled_u)
        value_portion = jnp.einsum("i,irc->rc", weights, jnp.log(kernel_u.astype(jnp.float32)))
        barycenter = jnp.exp(lax.psum(value_portion, "img") / total_weight)
        latest_multiplier = barycenter[None] / kernel_u.astype(jnp.float32)
    return (barycenter, latest_multiplier)


def solution(mesh):
    placed = (P("img", "slab", None), P("img", "slab", None), P("img"), P(), P())
    return jax.shard_map(
        per_device,
        mesh=mesh,
        in_specs=placed,
        out_specs=(P("slab", None), P("img", "slab", None)),
        check_vma=False,
    )
```

profile of v0, /device:TPU:0, one launch (start us, length us, event | category | flops | bytes accessed | tf_op | source)
XLA Modules:
  0.0 2068.6 jit_solution(6369687439953317268)
XLA Ops:
  77.7 49.0 %reduce.1 = bf16[3072,768]{1,0:T(8,128)(2,1)} reduce(bf16[3072,1,768]{2,1,0:T(2,128)(2,1)} %bitcast.287, bf16[]{:T(256)} %broadcast.49), dimensions={1}, to_apply=%bitcast.273.reduce_sub_computation | reduce | bytes 9437186
  132.1 61.0 %all_to_all.108 = bf16[4,2,294912]{2,1,0:T(2,128)(2,1)} all-to-all(bf16[4,2,294912]{2,1,0:T(2,128)(2,1)} %reshape.244), channel_id=1, replica_groups=mesh['img'=8,'slab'=4] {'slab'}, dimensions={0} | all-to-all | bytes 9437184 | tf_op jit(solution)/shard_map/all_to_all | solution.py:61
  269.0 49.2 %reduce.2 = bf16[3072,768]{1,0:T(8,128)(2,1)} reduce(bf16[3072,1,768]{2,1,0:T(2,128)(2,1)} %bitcast.290, bf16[]{:T(256)} %broadcast.49), dimensions={1}, to_apply=%bitcast.272.reduce_sub_computation | reduce | bytes 9437186
  338.2 42.8 %all-to-all-done.1 = bf16[4,2,294912]{2,1,0:T(2,128)(2,1)} async-done(((bf16[4,2,294912]{2,1,0:T(2,128)(2,1)}), bf16[4,2,294912]{2,1,0:T(2,128)(2,1)}, u32[]{:S(2)}, u32[]{:S(2)}) %all-to-all-start.1) | async-done | bytes 4718624 | tf_op jit(solution)/shard_map/all_to_all | solution.py:64
  389.0 23.5 %copy.138 = f32[1,4,768,768]{2,3,1,0:T(8,128)} copy(bf16[1,4,768,768]{3,0,2,1:T(2,128)(2,1)} %bitcast.291) | data formatting | bytes 14155776 | tf_op jit(solution)/shard_map/convert_element_type | solution.py:70
  478.4 49.4 %reduce.3 = bf16[3072,768]{1,0:T(8,128)(2,1)} reduce(bf16[3072,1,768]{2,1,0:T(2,128)(2,1)} %bitcast.292, bf16[]{:T(256)} %broadcast.49), dimensions={1}, to_apply=%bitcast.271.reduce_sub_computation | reduce | bytes 9437186
  533.1 58.9 %all_to_all.109 = bf16[4,2,294912]{2,1,0:T(2,128)(2,1)} all-to-all(bf16[4,2,294912]{2,1,0:T(2,128)(2,1)} %reshape.248), channel_id=1, replica_groups=mesh['img'=8,'slab'=4] {'slab'}, dimensions={0} | all-to-all | bytes 9437184 | tf_op jit(solution)/shard_map/all_to_all | solution.py:61
  667.7 49.1 %reduce.4 = bf16[3072,768]{1,0:T(8,128)(2,1)} reduce(bf16[3072,1,768]{2,1,0:T(2,128)(2,1)} %bitcast.294, bf16[]{:T(256)} %broadcast.49), dimensions={1}, to_apply=%bitcast.270.reduce_sub_computation | reduce | bytes 9437186
  727.9 50.3 %all-to-all-done.3 = bf16[4,2,294912]{2,1,0:T(2,128)(2,1)} async-done(((bf16[4,2,294912]{2,1,0:T(2,128)(2,1)}), bf16[4,2,294912]{2,1,0:T(2,128)(2,1)}, u32[]{:S(2)}, u32[]{:S(2)}) %all-to-all-start.3) | async-done | bytes 4718624 | tf_op jit(solution)/shard_map/all_to_all | solution.py:64
  801.7 23.3 %copy.145 = f32[1,4,768,768]{2,3,1,0:T(8,128)} copy(f32[1,4,768,768]{3,0,2,1:T(1,128)} %bitcast.302) | data formatting | bytes 18874368 | tf_op jit(solution)/shard_map/i,irc->rc/dot_general | solution.py:72
  841.9 23.6 %copy.146 = f32[1,4,768,768]{2,3,1,0:T(8,128)} copy(bf16[1,4,768,768]{3,0,2,1:T(2,128)(2,1)} %bitcast.274) | data formatting | bytes 14155776 | tf_op jit(solution)/shard_map/convert_element_type | solution.py:72
  865.5 155.0 %all-reduce.11.cloned.1.call-done = f32[768,3072]{0,1:T(8,128)} async-done(((f32[768,3072]{0,1:T(8,128)}), f32[768,3072]{0,1:T(8,128)}) %all-reduce.11.cloned.1.call-update) | async-done | bytes 9437200 | tf_op jit(solution)/shard_map/psum | solution.py:73
  1086.8 49.4 %reduce.5 = bf16[3072,768]{1,0:T(8,128)(2,1)} reduce(bf16[3072,1,768]{2,1,0:T(2,128)(2,1)} %bitcast.295, bf16[]{:T(256)} %broadcast.49), dimensions={1}, to_apply=%bitcast.269.reduce_sub_computation | reduce | bytes 9437186
  1141.6 59.5 %all_to_all.110 = bf16[4,2,294912]{2,1,0:T(2,128)(2,1)} all-to-all(bf16[4,2,294912]{2,1,0:T(2,128)(2,1)} %reshape.252), channel_id=1, replica_groups=mesh['img'=8,'slab'=4] {'slab'}, dimensions={0} | all-to-all | bytes 9437184 | tf_op jit(solution)/shard_map/all_to_all | solution.py:61
  1276.9 49.1 %reduce.6 = bf16[3072,768]{1,0:T(8,128)(2,1)} reduce(bf16[3072,1,768]{2,1,0:T(2,128)(2,1)} %bitcast.297, bf16[]{:T(256)} %broadcast.49), dimensions={1}, to_apply=%bitcast.268.reduce_sub_computation | reduce | bytes 9437186
  1331.4 58.2 %all_to_all.111 = bf16[4,2,294912]{2,1,0:T(2,128)(2,1)} all-to-all(bf16[4,2,294912]{2,1,0:T(2,128)(2,1)} %reshape.254), channel_id=1, replica_groups=mesh['img'=8,'slab'=4] {'slab'}, dimensions={0} | all-to-all | bytes 9437184 | tf_op jit(solution)/shard_map/all_to_all | solution.py:64
  1397.6 23.5 %copy.152 = f32[1,4,768,768]{2,3,1,0:T(8,128)} copy(bf16[1,4,768,768]{3,0,2,1:T(2,128)(2,1)} %bitcast.298) | data formatting | bytes 14155776 | tf_op jit(solution)/shard_map/convert_element_type | solution.py:70
  1486.9 49.4 %reduce.7 = bf16[3072,768]{1,0:T(8,128)(2,1)} reduce(bf16[3072,1,768]{2,1,0:T(2,128)(2,1)} %bitcast.299, bf16[]{:T(256)} %broadcast.49), dimensions={1}, to_apply=%bitcast.267.reduce_sub_computation | reduce | bytes 9437186
  1541.8 56.8 %all_to_all.112 = bf16[4,2,294912]{2,1,0:T(2,128)(2,1)} all-to-all(bf16[4,2,294912]{2,1,0:T(2,128)(2,1)} %reshape.256), channel_id=1, replica_groups=mesh['img'=8,'slab'=4] {'slab'}, dimensions={0} | all-to-all | bytes 9437184 | tf_op jit(solution)/shard_map/all_to_all | solution.py:61
  1674.4 49.2 %reduce.8 = bf16[3072,768]{1,0:T(8,128)(2,1)} reduce(bf16[3072,1,768]{2,1,0:T(2,128)(2,1)} %bitcast.288, bf16[]{:T(256)} %broadcast.49), dimensions={1}, to_apply=%bitcast.266.reduce_sub_computation | reduce | bytes 9437186
  1729.0 55.4 %all_to_all.113 = bf16[4,2,294912]{2,1,0:T(2,128)(2,1)} all-to-all(bf16[4,2,294912]{2,1,0:T(2,128)(2,1)} %reshape.258), channel_id=1, replica_groups=mesh['img'=8,'slab'=4] {'slab'}, dimensions={0} | all-to-all | bytes 9437184 | tf_op jit(solution)/shard_map/all_to_all | solution.py:64
  1807.7 23.3 %copy.159 = f32[1,4,768,768]{2,3,1,0:T(8,128)} copy(f32[1,4,768,768]{3,0,2,1:T(1,128)} %bitcast.301) | data formatting | bytes 18874368 | tf_op jit(solution)/shard_map/i,irc->rc/dot_general | solution.py:72
  1831.0 23.5 %copy.160 = f32[1,4,768,768]{2,3,1,0:T(8,128)} copy(bf16[1,4,768,768]{3,0,2,1:T(2,128)(2,1)} %bitcast.275) | data formatting | bytes 14155776 | tf_op jit(solution)/shard_map/convert_element_type | solution.py:72
  1854.5 172.9 %all-reduce.13.cloned.1.call-done = f32[768,3072]{0,1:T(8,128)} async-done(((f32[768,3072]{0,1:T(8,128)}), f32[768,3072]{0,1:T(8,128)}) %all-reduce.13.cloned.1.call-update) | async-done | bytes 9437200 | tf_op jit(solution)/shard_map/psum | solution.py:73
  (136 shorter events, 748.3 us)
Async XLA Ops:
  15.6 6.9 copy-start.16
  26.3 18.9 copy-start
  26.3 8.9 copy-start.12
  214.4 7.8 copy-start.8
  222.3 3.8 copy-start.1
  323.6 57.3 %all-to-all-start.1 = ((bf16[4,2,294912]{2,1,0:T(2,128)(2,1)}), bf16[4,2,294912]{2,1,0:T(2,128)(2,1)}, u32[]{:S(2)}, u32[]{:S(2)}) async-start(bf16[4,2,294912]{2,1,0:T(2,128)(2,1)} %reshape.246), calls=%async_computation.1 | async-start | bytes 9437184 | tf_op jit(solution)/shard_map/all_to_all | solution.py:64
  429.2 7.7 copy-start.2
  429.2 7.7 copy-start.13
  613.3 7.7 copy-start.9
  621.0 3.8 copy-start.3
  722.3 56.0 %all-to-all-start.3 = ((bf16[4,2,294912]{2,1,0:T(2,128)(2,1)}), bf16[4,2,294912]{2,1,0:T(2,128)(2,1)}, u32[]{:S(2)}, u32[]{:S(2)}) async-start(bf16[4,2,294912]{2,1,0:T(2,128)(2,1)} %reshape.250), calls=%async_computation.3 | async-start | bytes 9437184 | tf_op jit(solution)/shard_map/all_to_all | solution.py:64
  727.2 293.3 %all-reduce.11.cloned.1.call-start = ((), (), s32[]{:S(2)}) async-start(), calls=%async_computation.8 | async-start | bytes 18874368 | tf_op jit(solution)/shard_map/psum | solution.py:73
  824.9 1202.4 %all-reduce.13.cloned.1.call-start = ((), (), s32[]{:S(2)}) async-start(), calls=%async_computation.9 | async-start | bytes 18874368 | tf_op jit(solution)/shard_map/psum | solution.py:73
  1037.6 7.7 copy-start.4
  1037.6 7.7 copy-start.14
  1222.4 7.7 copy-start.10
  1230.1 3.8 copy-start.5
  1437.7 7.8 copy-start.6
  1437.7 7.8 copy-start.15
  1619.9 7.8 copy-start.11
  1627.7 3.8 copy-start.7
Sparse Core Ops, SparseCore 0:
  825.1 195.3 all-reduce.10
  1831.1 196.2 all-reduce.12
where the time goes:
time: 2080 us; the launch traced here: 2070 us
  other arithmetic  474 us (23%)
  local copies, waits for them, and re-layouts  458 us (22%)
  waiting for transfers between devices  421 us (20%)
  blocking collectives  367 us (18%)
  matrix products  324 us (16%)
    unnamed x8, other arithmetic  394 us
    psum x2, waiting for transfers between devices, per_device(): barycenter = jnp.exp(lax.psum(value_portion, 'img') / total_weight)  328 us
    all_to_all x4, blocking collectives, apply_kernel(): lax.all_to_all(inner, 'slab', split_axis=2, concat_axis=1, tiled=True)  236 us
    unnamed x60, local copies, waits for them, and re-layouts  174 us
    dot_general x20, matrix products, rows_pass(): lax.dot_general(terms[:, offset], split[offset:offset + block_stack], (((...  165 us
    dot_general x20, matrix products, column_sweep(): lax.dot_general(padded[offset:offset + block_stack], terms[:, offset], ((...  160 us
    all_to_all x2, blocking collectives, apply_kernel(): lax.all_to_all(result, 'slab', split_axis=1, concat_axis=2, tiled=True)  114 us
    all_to_all x2, waiting for transfers between devices, apply_kernel(): lax.all_to_all(result, 'slab', split_axis=1, concat_axis=2, tiled=True)  93.1 us
  transfers between devices with their start and end apart: 4, of which 4 were waited for; matrix products, arithmetic and copies ran while one was open for 3% of the time, Pallas kernels for 0%

commit v1 on v0

--- a/solution.py
+++ b/solution.py
@@ -58,7 +58,13 @@
 
     def apply_kernel(field):
         inner = column_sweep(field, terms).astype(jnp.bfloat16)
-        columns = lax.all_to_all(inner, "slab", split_axis=2, concat_axis=1, tiled=True)
+        r_now = lax.all_to_all(
+            jnp.stack(jnp.split(inner, lax.axis_size("slab"), axis=2)),
+            "slab",
+            split_axis=0,
+            concat_axis=0,
+        )
+        columns = jnp.concatenate(r_now, axis=1)
         padded = jnp.pad(columns, ((0, 0), (2 * width, 2 * width), (0, 0)))
         result = rows_pass(padded, terms).astype(jnp.bfloat16)
         return lax.all_to_all(result, "slab", split_axis=1, concat_axis=2, tiled=True)

time: 2080 us -> 1770 us (0.85)
  other arithmetic: 474 us -> 284 us
  local copies, waits for them, and re-layouts: 458 us -> 351 us
    unnamed x8 -> x4, other arithmetic: 394 us -> 196 us
    unnamed x60 -> x56, local copies, waits for them, and re-layouts: 174 us -> 116 us
    convert_element_type x4 -> x0, local copies, waits for them, and re-layouts: 38.6 us -> none  [apply_kernel(): inner = column_sweep(field, terms).astype(jnp.bfloat16)]
    all_to_all x4 -> x0, local copies, waits for them, and re-layouts: 26.4 us -> none  [apply_kernel(): lax.all_to_all(inner, 'slab', split_axis=2, concat_axis=1, tiled=True)]
where the time goes in v1:
time: 1770 us; the launch traced here: 1750 us
  waiting for transfers between devices  419 us (24%)
  blocking collectives  357 us (20%)
  local copies, waits for them, and re-layouts  351 us (20%)
  matrix products  314 us (18%)
  other arithmetic  284 us (16%)
    psum x2, waiting for transfers between devices, per_device(): barycenter = jnp.exp(lax.psum(value_portion, 'img') / total_weight)  326 us
    all_to_all x4, blocking collectives, apply_kernel(): lax.all_to_all(jnp.stack(jnp.split(inner, lax.axis_size('slab'), axis=2))...  226 us
    unnamed x4, other arithmetic  196 us
    dot_general x20, matrix products, column_sweep(): lax.dot_general(padded[offset:offset + block_stack], terms[:, offset], ((...  160 us
    dot_general x20, matrix products, rows_pass(): lax.dot_general(terms[:, offset], split[offset:offset + block_stack], (((...  154 us
    unnamed x56, local copies, waits for them, and re-layouts  116 us
    all_to_all x2, blocking collectives, apply_kernel(): lax.all_to_all(result, 'slab', split_axis=1, concat_axis=2, tiled=True)  113 us
    all_to_all x2, waiting for transfers between devices, apply_kernel(): lax.all_to_all(result, 'slab', split_axis=1, concat_axis=2, tiled=True)  92.5 us
  transfers between devices with their start and end apart: 4, of which 4 were waited for; matrix products, arithmetic and copies ran while one was open for 3% of the time, Pallas kernels for 0%

profile of v1, /device:TPU:0, one launch (start us, length us, event | category | flops | bytes accessed | tf_op | source)
XLA Modules:
  0.0 1749.9 jit_solution(4947922025691061084)
XLA Ops:
  79.1 59.0 %all_to_all.56 = bf16[4,1,768,768]{3,2,1,0:T(8,128)(2,1)S(1)} all-to-all(bf16[4,1,768,768]{3,2,1,0:T(8,128)(2,1)S(1)} %pad_maximum_fusion), channel_id=1, replica_groups=mesh['img'=8,'slab'=4] {'slab'}, dimensions={0} | all-to-all | bytes 9437184 | tf_op jit(solution)/shard_map/all_to_all | solution.py:61
  161.8 18.2 %add_convert_fusion.6 = bf16[24,128,768]{2,1,0:T(8,128)(2,1)} fusion(f32[24,128,768]{2,1,0:T(8,128)} %fusion.67, f32[24,128,768]{2,1,0:T(8,128)} %fusion.63, f32[24,128,768]{2,1,0:T(8,128)} %fusion.55, f32[24,128,768]{2,1,0:T(8,128)} %fusion.59, bf16[24,128,768]{2,1,0:T(8,128)(2,1)} %bitcast.288, bf16[24,5,128,128]{3,2,1,0:T(8,128)(2,1)} %copy-done), kind=kOutput, calls=%fused_computation.21 | convolution fusion | flops 615776256 | bytes 47972352 | tf_op jit(solution)/shard_map/dot_general | solution.py:43
  190.0 49.0 %reduce.1 = bf16[3072,768]{1,0:T(8,128)(2,1)} reduce(bf16[3072,1,768]{2,1,0:T(2,128)(2,1)} %bitcast.275, bf16[]{:T(256)} %broadcast.49), dimensions={1}, to_apply=%bitcast.261.reduce_sub_computation | reduce | bytes 9437186
  259.2 42.2 %all-to-all-done.1 = bf16[4,2,294912]{2,1,0:T(2,128)(2,1)} async-done(((bf16[4,2,294912]{2,1,0:T(2,128)(2,1)}), bf16[4,2,294912]{2,1,0:T(2,128)(2,1)}, u32[]{:S(2)}, u32[]{:S(2)}) %all-to-all-start.1) | async-done | bytes 4718624 | tf_op jit(solution)/shard_map/all_to_all | solution.py:70
  309.4 23.6 %copy.99 = f32[1,4,768,768]{2,3,1,0:T(8,128)} copy(bf16[1,4,768,768]{3,0,2,1:T(2,128)(2,1)} %bitcast.277) | data formatting | bytes 14155776 | tf_op jit(solution)/shard_map/convert_element_type | solution.py:76
  401.3 56.2 %all_to_all.57 = bf16[4,1,768,768]{3,2,1,0:T(8,128)(2,1)S(1)} all-to-all(bf16[4,1,768,768]{3,2,1,0:T(8,128)(2,1)S(1)} %pad_maximum_fusion.1), channel_id=1, replica_groups=mesh['img'=8,'slab'=4] {'slab'}, dimensions={0} | all-to-all | bytes 9437184 | tf_op jit(solution)/shard_map/all_to_all | solution.py:61
  481.1 18.2 %add_convert_fusion.4 = bf16[24,128,768]{2,1,0:T(8,128)(2,1)} fusion(f32[24,128,768]{2,1,0:T(8,128)} %fusion.66, f32[24,128,768]{2,1,0:T(8,128)} %fusion.62, f32[24,128,768]{2,1,0:T(8,128)} %fusion.54, f32[24,128,768]{2,1,0:T(8,128)} %fusion.58, bf16[24,128,768]{2,1,0:T(8,128)(2,1)} %bitcast.289, bf16[24,5,128,128]{3,2,1,0:T(8,128)(2,1)} %copy-done), kind=kOutput, calls=%fused_computation.19 | convolution fusion | flops 615776256 | bytes 47972352 | tf_op jit(solution)/shard_map/dot_general | solution.py:43
  508.8 49.1 %reduce.2 = bf16[3072,768]{1,0:T(8,128)(2,1)} reduce(bf16[3072,1,768]{2,1,0:T(2,128)(2,1)} %bitcast.278, bf16[]{:T(256)} %broadcast.49), dimensions={1}, to_apply=%bitcast.260.reduce_sub_computation | reduce | bytes 9437186
  569.0 50.3 %all-to-all-done.3 = bf16[4,2,294912]{2,1,0:T(2,128)(2,1)} async-done(((bf16[4,2,294912]{2,1,0:T(2,128)(2,1)}), bf16[4,2,294912]{2,1,0:T(2,128)(2,1)}, u32[]{:S(2)}, u32[]{:S(2)}) %all-to-all-start.3) | async-done | bytes 4718624 | tf_op jit(solution)/shard_map/all_to_all | solution.py:70
  642.7 23.3 %copy.107 = f32[1,4,768,768]{2,3,1,0:T(8,128)} copy(f32[1,4,768,768]{3,0,2,1:T(1,128)} %bitcast.282) | data formatting | bytes 18874368 | tf_op jit(solution)/shard_map/i,irc->rc/dot_general | solution.py:78
  683.4 23.6 %copy.108 = f32[1,4,768,768]{2,3,1,0:T(8,128)} copy(bf16[1,4,768,768]{3,0,2,1:T(2,128)(2,1)} %bitcast.262) | data formatting | bytes 14155776 | tf_op jit(solution)/shard_map/convert_element_type | solution.py:78
  707.0 155.0 %all-reduce.11.cloned.1.call-done = f32[768,3072]{0,1:T(8,128)} async-done(((f32[768,3072]{0,1:T(8,128)}), f32[768,3072]{0,1:T(8,128)}) %all-reduce.11.cloned.1.call-update) | async-done | bytes 9437200 | tf_op jit(solution)/shard_map/psum | solution.py:79
  930.8 57.4 %all_to_all.58 = bf16[4,1,768,768]{3,2,1,0:T(8,128)(2,1)S(1)} all-to-all(bf16[4,1,768,768]{3,2,1,0:T(8,128)(2,1)S(1)} %pad_maximum_fusion.2), channel_id=1, replica_groups=mesh['img'=8,'slab'=4] {'slab'}, dimensions={0} | all-to-all | bytes 9437184 | tf_op jit(solution)/shard_map/all_to_all | solution.py:61
  1011.8 18.2 %add_convert_fusion.2 = bf16[24,128,768]{2,1,0:T(8,128)(2,1)} fusion(f32[24,128,768]{2,1,0:T(8,128)} %fusion.65, f32[24,128,768]{2,1,0:T(8,128)} %fusion.61, f32[24,128,768]{2,1,0:T(8,128)} %fusion.53, f32[24,128,768]{2,1,0:T(8,128)} %fusion.57, bf16[24,128,768]{2,1,0:T(8,128)(2,1)} %bitcast.290, bf16[24,5,128,128]{3,2,1,0:T(8,128)(2,1)} %copy-done), kind=kOutput, calls=%fused_computation.16 | convolution fusion | flops 615776256 | bytes 47972352 | tf_op jit(solution)/shard_map/dot_general | solution.py:43
  1039.5 49.1 %reduce.3 = bf16[3072,768]{1,0:T(8,128)(2,1)} reduce(bf16[3072,1,768]{2,1,0:T(2,128)(2,1)} %bitcast.279, bf16[]{:T(256)} %broadcast.49), dimensions={1}, to_apply=%bitcast.259.reduce_sub_computation | reduce | bytes 9437186
  1093.9 58.0 %all_to_all.59 = bf16[4,2,294912]{2,1,0:T(2,128)(2,1)} all-to-all(bf16[4,2,294912]{2,1,0:T(2,128)(2,1)} %reshape.264), channel_id=1, replica_groups=mesh['img'=8,'slab'=4] {'slab'}, dimensions={0} | all-to-all | bytes 9437184 | tf_op jit(solution)/shard_map/all_to_all | solution.py:70
  1160.0 23.6 %copy.115 = f32[1,4,768,768]{2,3,1,0:T(8,128)} copy(bf16[1,4,768,768]{3,0,2,1:T(2,128)(2,1)} %bitcast.280) | data formatting | bytes 14155776 | tf_op jit(solution)/shard_map/convert_element_type | solution.py:76
  1251.9 53.8 %all_to_all.60 = bf16[4,1,768,768]{3,2,1,0:T(8,128)(2,1)S(1)} all-to-all(bf16[4,1,768,768]{3,2,1,0:T(8,128)(2,1)S(1)} %pad_maximum_fusion.3), channel_id=1, replica_groups=mesh['img'=8,'slab'=4] {'slab'}, dimensions={0} | all-to-all | bytes 9437184 | tf_op jit(solution)/shard_map/all_to_all | solution.py:61
  1329.3 18.2 %add_convert_fusion = bf16[24,128,768]{2,1,0:T(8,128)(2,1)} fusion(f32[24,128,768]{2,1,0:T(8,128)} %fusion.64, f32[24,128,768]{2,1,0:T(8,128)} %fusion.60, f32[24,128,768]{2,1,0:T(8,128)} %fusion.52, f32[24,128,768]{2,1,0:T(8,128)} %fusion.56, bf16[24,128,768]{2,1,0:T(8,128)(2,1)} %bitcast.287, bf16[24,5,128,128]{3,2,1,0:T(8,128)(2,1)} %copy-done), kind=kOutput, calls=%fused_computation.14 | convolution fusion | flops 615776256 | bytes 47972352 | tf_op jit(solution)/shard_map/dot_general | solution.py:43
  1357.0 49.2 %reduce.4 = bf16[3072,768]{1,0:T(8,128)(2,1)} reduce(bf16[3072,1,768]{2,1,0:T(2,128)(2,1)} %bitcast.276, bf16[]{:T(256)} %broadcast.49), dimensions={1}, to_apply=%bitcast.258.reduce_sub_computation | reduce | bytes 9437186
  1411.6 55.5 %all_to_all.61 = bf16[4,2,294912]{2,1,0:T(2,128)(2,1)} all-to-all(bf16[4,2,294912]{2,1,0:T(2,128)(2,1)} %reshape.266), channel_id=1, replica_groups=mesh['img'=8,'slab'=4] {'slab'}, dimensions={0} | all-to-all | bytes 9437184 | tf_op jit(solution)/shard_map/all_to_all | solution.py:70
  1490.4 23.2 %copy.123 = f32[1,4,768,768]{2,3,1,0:T(8,128)} copy(f32[1,4,768,768]{3,0,2,1:T(1,128)} %bitcast.281) | data formatting | bytes 18874368 | tf_op jit(solution)/shard_map/i,irc->rc/dot_general | solution.py:78
  1513.7 23.4 %copy.124 = f32[1,4,768,768]{2,3,1,0:T(8,128)} copy(bf16[1,4,768,768]{3,0,2,1:T(2,128)(2,1)} %bitcast.263) | data formatting | bytes 14155776 | tf_op jit(solution)/shard_map/convert_element_type | solution.py:78
  1537.1 171.2 %all-reduce.13.cloned.1.call-done = f32[768,3072]{0,1:T(8,128)} async-done(((f32[768,3072]{0,1:T(8,128)}), f32[768,3072]{0,1:T(8,128)}) %all-reduce.13.cloned.1.call-update) | async-done | bytes 9437200 | tf_op jit(solution)/shard_map/psum | solution.py:79
  (128 shorter events, 566.0 us)
Async XLA Ops:
  15.6 6.9 copy-start.12
  26.3 18.9 %copy-start = (bf16[24,5,128,128]{3,2,1,0:T(8,128)(2,1)}, bf16[24,5,128,128]{3,2,1,0:T(8,128)(2,1)S(1)}, u32[]{:S(2)}) copy-start(bf16[24,5,128,128]{3,2,1,0:T(8,128)(2,1)S(1)} %select_reduce_fusion) | copy-start | bytes 11796484
  26.3 8.9 copy-start.8
  79.1 59.0 %copy-start.1 = (bf16[24,5,128,128]{3,2,1,0:T(8,128)(2,1)S(1)}, bf16[24,5,128,128]{3,2,1,0:T(8,128)(2,1)}, u32[]{:S(2)}) copy-start(bf16[24,5,128,128]{3,2,1,0:T(8,128)(2,1)} %copy-done) | copy-start | bytes 11796484
  244.5 56.9 %all-to-all-start.1 = ((bf16[4,2,294912]{2,1,0:T(2,128)(2,1)}), bf16[4,2,294912]{2,1,0:T(2,128)(2,1)}, u32[]{:S(2)}, u32[]{:S(2)}) async-start(bf16[4,2,294912]{2,1,0:T(2,128)(2,1)} %reshape.260), calls=%async_computation.1 | async-start | bytes 9437184 | tf_op jit(solution)/shard_map/all_to_all | solution.py:70
  349.6 7.7 copy-start.2
  349.6 7.7 copy-start.9
  401.3 56.2 %copy-start.3 = (bf16[24,5,128,128]{3,2,1,0:T(8,128)(2,1)S(1)}, bf16[24,5,128,128]{3,2,1,0:T(8,128)(2,1)}, u32[]{:S(2)}) copy-start(bf16[24,5,128,128]{3,2,1,0:T(8,128)(2,1)} %copy-done) | copy-start | bytes 11796484
  563.3 56.0 %all-to-all-start.3 = ((bf16[4,2,294912]{2,1,0:T(2,128)(2,1)}), bf16[4,2,294912]{2,1,0:T(2,128)(2,1)}, u32[]{:S(2)}, u32[]{:S(2)}) async-start(bf16[4,2,294912]{2,1,0:T(2,128)(2,1)} %reshape.262), calls=%async_computation.3 | async-start | bytes 9437184 | tf_op jit(solution)/shard_map/all_to_all | solution.py:70
  568.3 293.7 %all-reduce.11.cloned.1.call-start = ((), (), s32[]{:S(2)}) async-start(), calls=%async_computation.8 | async-start | bytes 18874368 | tf_op jit(solution)/shard_map/psum | solution.py:79
  666.1 1042.3 %all-reduce.13.cloned.1.call-start = ((), (), s32[]{:S(2)}) async-start(), calls=%async_computation.9 | async-start | bytes 18874368 | tf_op jit(solution)/shard_map/psum | solution.py:79
  879.1 7.7 copy-start.4
  879.1 7.7 copy-start.10
  930.8 57.4 %copy-start.5 = (bf16[24,5,128,128]{3,2,1,0:T(8,128)(2,1)S(1)}, bf16[24,5,128,128]{3,2,1,0:T(8,128)(2,1)}, u32[]{:S(2)}) copy-start(bf16[24,5,128,128]{3,2,1,0:T(8,128)(2,1)} %copy-done) | copy-start | bytes 11796484
  1200.2 7.8 copy-start.6
  1200.2 7.8 copy-start.11
  1251.9 53.8 %copy-start.7 = (bf16[24,5,128,128]{3,2,1,0:T(8,128)(2,1)S(1)}, bf16[24,5,128,128]{3,2,1,0:T(8,128)(2,1)}, u32[]{:S(2)}) copy-start(bf16[24,5,128,128]{3,2,1,0:T(8,128)(2,1)} %copy-done) | copy-start | bytes 11796484
Sparse Core Ops, SparseCore 0:
  666.2 195.7 all-reduce.10
  1513.8 194.4 all-reduce.12
